TPU v7x, 32 devices: a whole 2x2x4 slice. The times are simulated.
32 devices in a mesh: groups: 2 (over y), lon: 8 (over z, x), lat: 2 (over core).
Axes of the slice: x: 2, y: 2, z: 4, core: 2. Of those that a mesh axis runs over, the one named last changes fastest.
Arguments:
- acts: bfloat16 [4, 96, 256, 256], P('groups', 'lat', 'lon'), parts along dimension 0, may hold values from -6 to 6
- rates: int32 [256], replicated, may hold values from 1 to 4, as said below
- dw_kernel: bfloat16 [9, 256], replicated, may hold values from -2 to 2
- pw_weight: bfloat16 [256, 256], replicated, may hold values from -0.375 to 0.375
- head_weight: bfloat16 [256, 227], replicated, may hold values from -0.375 to 0.375
- teacher_tiles: bfloat16 [512, 8, 227], P(('groups', 'lon', 'lat')), parts along dimension 0, may hold values from -6 to 6
- tile_dest: int32 [512, 1], P(('groups', 'lon', 'lat')), parts along dimension 0, may hold values from 0 to 15; in each aligned block of 16 rows (0 to 15, 16 to 31, ...) at most 2 rows name the same one
- tile_start: int32 [512], P(('groups', 'lon', 'lat')), parts along dimension 0, may hold values from 0 to 3064, as said below
- tile_count: int32 [512], P(('groups', 'lon', 'lat')), parts along dimension 0, may hold values from 1 to 8
Outputs:
- grad_dw: float32 [18, 256], P('groups'), parts along dimension 0
- grad_pw: float32 [512, 256], P('groups'), parts along dimension 0
- grad_head: float32 [512, 227], P('groups'), parts along dimension 0
- mse: float32 [2], P('groups'), parts along dimension 0
There are 2 independent parts, one for each index of `groups`. A program takes and returns all parts, laid end to end along the dimension named above; an argument that names none is the same for every part. Nothing has to cross between parts.
Inputs may be any that keep to these rules, and one draw needn't show every extreme that they name: The channels form 4 contiguous groups of 64 channels; all channels of a group share one rate, and the groups take the rates 1 to 4, each once, in an order that varies. `tile_dest`: among the 16 tiles of one teacher partition no destination is named more than 2 times. A tile's 8 cells lie in one row of one sample of its destination's block: tile_start mod 32 is at most 24.
All inputs are finite; a program needn't handle non-finite values.
Results may differ from a plain program's by a relative error of at most 0.0045.
Values may be sent and summed in bfloat16 or wider, within the bound.
No kernel may reach another device: no remote copies, remote signals or barrier semaphores. Data moves between devices by JAX's collectives and lax.ppermute only.
A program may use at most 64 MiB of HBM per device.

v0:
```python
import jax
import jax.numpy as jnp
from jax import lax
from jax.sharding import PartitionSpec as P

DMAX = 4
TILE = 8
CAP = 2


def padded_2(cells, sides, width, closed):
    for axis, dim in sides:
        count = lax.axis_size(axis)
        ends = count if closed else count - 1
        head = lax.slice_in_dim(cells, 0, width, axis=dim)
        tail = lax.slice_in_dim(cells, cells.shape[dim] - width, cells.shape[dim], axis=dim)
        cells = jnp.concatenate(
            [
                lax.ppermute(tail, axis, [(i, (i + 1) % count) for i in range(ends)]),
                cells,
                lax.ppermute(head, axis, [((i + 1) % count, i) for i in range(ends)]),
            ],
            axis=dim,
        )
    return cells


def tap_window(group_in, rate, tap_index, band_rows, block_cols):
    row_start = DMAX + (tap_index // 3 - 1) * rate
    col_start = DMAX + (tap_index % 3 - 1) * rate
    zero = jnp.int32(0)
    sizes = (group_in.shape[0], band_rows, block_cols, group_in.shape[3])
    return lax.dynamic_slice(group_in, (zero, row_start, col_start, zero), sizes)


def dilated(padded, kernel, rates, band_rows, block_cols):
    width = padded.shape[-1]
    group_width = width // DMAX
    outputs = []
    for group in range(DMAX):
        low = group * group_width
        group_in = padded[..., low : low + group_width]
        rate = rates[low]
        accum_sum = None
        for tap_index in range(9):
            window = tap_window(group_in, rate, tap_index, band_rows, block_cols)
            term = window.astype(jnp.float32) * kernel[tap_index, low : low + group_width]
            accum_sum = term if accum_sum is None else accum_sum + term
        outputs.append(accum_sum)
    return jnp.concatenate(outputs, axis=-1)


def dilated_grad(padded, grad_z, rates, band_rows, block_cols):
    width = padded.shape[-1]
    group_width = width // DMAX
    columns = []
    for group in range(DMAX):
        low = group * group_width
        group_in = padded[..., low : low + group_width]
        group_grad = grad_z[..., low : low + group_width]
        rate = rates[low]
        tap_sums = []
        for tap_index in range(9):
            window = tap_window(group_in, rate, tap_index, band_rows, block_cols)
            tap_sums.append(
                jnp.sum((window.astype(jnp.float32) * group_grad).reshape(-1, group_width), axis=0)
            )
        columns.append(jnp.stack(tap_sums, axis=0))
    return jnp.concatenate(columns, axis=1)


def local(
    acts, rates, dw_kernel, pw_weight, head_weight, teacher_tiles, tile_dest, tile_start, tile_count
):
    micro_batch, band_rows, block_cols, width = acts.shape
    teach_width = head_weight.shape[1]
    lat_index = lax.axis_index("lat")
    lat_count = lax.axis_size("lat")
    lon_count = lax.axis_size("lon")
    devices = lon_count * lat_count
    lon_padded = padded_2(acts, (("lon", 2),), DMAX, True)
    padded = padded_2(lon_padded, (("lat", 1),), DMAX, False)
    kernel = dw_kernel.astype(jnp.float32)
    depthwise_out = dilated(padded, kernel, rates, band_rows, block_cols).astype(jnp.bfloat16)
    depth_flat = depthwise_out.reshape(-1, width)
    preact = jnp.dot(depth_flat, pw_weight, preferred_element_type=jnp.float32)
    block_flat = (acts.reshape(-1, width).astype(jnp.float32) + jax.nn.silu(preact)).astype(
        jnp.bfloat16
    )
    tiles_here = teacher_tiles.shape[0]
    destination = tile_dest[:, 0]
    positions = jnp.arange(tiles_here, dtype=jnp.int32)
    same_dest = destination[:, None] == destination[None, :]
    earlier = positions[:, None] > positions[None, :]
    slot_rank = jnp.sum((same_dest & earlier).astype(jnp.int32), axis=1)
    slot_index = destination * CAP + slot_rank
    send_tiles = (
        jnp.zeros((devices * CAP, TILE, teach_width), jnp.bfloat16)
        .at[slot_index]
        .set(teacher_tiles)
    )
    send_start = jnp.zeros((devices * CAP,), jnp.int32).at[slot_index].set(tile_start)
    send_count = jnp.zeros((devices * CAP,), jnp.int32).at[slot_index].set(tile_count)
    recv_tiles, recv_start, recv_count = (
        lax.all_to_all(send_tiles, ("lon", "lat"), split_axis=0, concat_axis=0, tiled=True),
        lax.all_to_all(send_start, ("lon", "lat"), split_axis=0, concat_axis=0, tiled=True),
        lax.all_to_all(send_count, ("lon", "lat"), split_axis=0, concat_axis=0, tiled=True),
    )
    offsets = jnp.arange(TILE, dtype=jnp.int32)
    cell_index = recv_start[:, None] + offsets[None, :]
    is_valid = offsets[None, :] < recv_count[:, None]
    inner_row = recv_start // block_cols % band_rows
    glob_row = lat_index * band_rows + inner_row
    area_weight = jnp.cos(
        jnp.pi * ((glob_row.astype(jnp.float32) + 0.5) / (band_rows * lat_count) - 0.5)
    )
    row_weight = jnp.where(is_valid, area_weight[:, None], jnp.float32(0.0)) / jnp.float32(
        devices * tiles_here * TILE
    )
    row_weight = row_weight.reshape(-1, 1)
    cell_flat = cell_index.reshape(-1)
    y_rows = block_flat[cell_flat]
    predicted = jnp.dot(y_rows, head_weight, preferred_element_type=jnp.float32)
    residual = predicted - recv_tiles.reshape(-1, teach_width).astype(jnp.float32)
    loss_sum = jnp.sum(row_weight * residual * residual)
    grad_pred = (2.0 * row_weight * residual).astype(jnp.bfloat16)
    grad_head = lax.dot_general(
        y_rows, grad_pred, (((0,), (0,)), ((), ())), preferred_element_type=jnp.float32
    )
    grad_rows = jnp.dot(grad_pred, head_weight.T, preferred_element_type=jnp.float32)
    grad_y = jnp.zeros((block_flat.shape[0], width), jnp.float32).at[cell_flat].add(grad_rows)
    sigmoid_u = jax.nn.sigmoid(preact)
    grad_u = (grad_y * sigmoid_u * (1.0 + preact * (1.0 - sigmoid_u))).astype(jnp.bfloat16)
    grad_pw = lax.dot_general(
        depth_flat, grad_u, (((0,), (0,)), ((), ())), preferred_element_type=jnp.float32
    )
    grad_z = jnp.dot(grad_u, pw_weight.T, preferred_element_type=jnp.float32).reshape(
        micro_batch, band_rows, block_cols, width
    )
    grad_dw = dilated_grad(padded, grad_z, rates, band_rows, block_cols)
    grad_dw, grad_pw, grad_head, loss_sum = lax.psum(
        (grad_dw, grad_pw, grad_head, loss_sum), ("lon", "lat")
    )
    return (grad_dw, grad_pw, grad_head, (loss_sum / teach_width).reshape(1))


def solution(mesh):
    in_specs = (
        P("groups", "lat", "lon", None),
        P(),
        P(),
        P(),
        P(),
        P(("groups", "lon", "lat"), None, None),
        P(("groups", "lon", "lat"), None),
        P(("groups", "lon", "lat")),
        P(("groups", "lon", "lat")),
    )
    out_specs = (P("groups", None), P("groups", None), P("groups", None), P("groups"))
    return jax.shard_map(local, mesh=mesh, in_specs=in_specs, out_specs=out_specs, check_vma=False)
```

profile of v0, /device:TPU:8, one launch (start us, length us, event | category | flops | bytes accessed | tf_op | source)
XLA Modules:
  0.0 212.1 jit_solution(15716888762554736010)
XLA Ops:
  7.2 1.0 convert_reduce_fusion
  8.2 0.7 fusion.86
  8.8 0.8 scatter_custom_fusion.1
  9.6 0.7 all_to_all.17
  10.3 6.3 %all-to-all-start.1 = ((s32[16,2,1]{1,2,0:T(1,128)}), s32[16,2,1]{1,2,0:T(1,128)S(1)}, u32[]{:S(2)}, u32[]{:S(2)}) async-start(s32[16,2,1]{1,2,0:T(1,128)} %bitcast.8), calls=%async_computation.1 | async-start | bytes 16384 | tf_op jit(solution)/shard_map/all_to_all | solution.py:107
  16.5 1.3 fusion.94
  17.8 1.5 collective-permute-start
  19.3 1.5 collective-permute-start.1
  20.8 1.4 fusion.95
  32.8 0.7 convert_element_type.185
  33.5 0.7 slice_bitcast_fusion.35
  34.2 0.8 scatter_custom_fusion
  35.1 0.7 all_to_all.15
  35.8 5.2 %all-to-all-start = ((s32[16,2,1]{1,2,0:T(1,128)}), s32[16,2,1]{1,2,0:T(1,128)S(1)}, u32[]{:S(2)}, u32[]{:S(2)}) async-start(s32[16,2,1]{1,2,0:T(1,128)} %bitcast.6), calls=%async_computation | async-start | bytes 16384 | tf_op jit(solution)/shard_map/all_to_all | solution.py:106
  41.0 0.7 broadcast_in_dim.15
  41.6 2.3 %scatter_fusion = bf16[32,8,227]{2,1,0:T(8,128)(2,1)} fusion(bf16[32,8,227]{2,1,0:T(8,128)(2,1)} %broadcast_in_dim.15, s32[16]{0:T(128)S(1)} %fusion.86, bf16[16,8,227]{2,1,0:T(8,128)(2,1)} %param.14), kind=kCustom, calls=%fused_computation.3 | custom fusion | bytes 174400 | tf_op jit(solution)/shard_map/scatter | solution.py:100
  43.9 0.6 broadcast.181
  44.5 0.6 reduce.43
  45.2 0.7 all-to-all-done
  45.9 5.4 %all-to-all-start.2 = ((bf16[32,8,227]{2,1,0:T(8,128)(2,1)}), bf16[32,8,227]{2,1,0:T(8,128)(2,1)S(1)}, u32[]{:S(2)}, u32[]{:S(2)}) async-start(bf16[32,8,227]{2,1,0:T(8,128)(2,1)} %scatter_fusion), calls=%async_computation.2 | async-start | bytes 262144 | tf_op jit(solution)/shard_map/all_to_all | solution.py:105
  51.4 0.6 reduce.42
  52.8 2.1 collective-permute-start.2
  54.9 1.3 collective-permute-start.3
  56.2 0.5 all-to-all-done.2
  56.9 1.3 collective-permute-done.3
  58.2 1.4 pad_maximum_fusion
  59.6 1.0 fusion.93
  60.6 0.3 copy-done.7
  61.0 3.5 %fusion.9 = bf16[2,48,32,64]{3,2,1,0:T(8,128)(2,1)S(1)} fusion(f32[64]{0:T(128)S(1)} %get-tuple-element.101, f32[64]{0:T(128)S(1)} %get-tuple-element.102, f32[64]{0:T(128)S(1)} %get-tuple-element.103, f32[64]{0:T(128)S(1)} %get-tuple-element.104, f32[64]{0:T(128)S(1)} %get-tuple-element.105, f32[64]{0:T(128)S(1)} %get-tuple-element.106, ...), kind=kLoop, calls=%fused_computation.90 | loop fusion | flops 5308416 | bytes 3934480 | tf_op jit(solution)/shard_map/convert.9
  64.6 3.1 %fusion.63 = bf16[2,48,32,64]{3,2,1,0:T(8,128)(2,1)S(1)} fusion(f32[64]{0:T(128)S(1)} %copy-done.22, f32[64]{0:T(128)S(1)} %copy-done.23, f32[64]{0:T(128)S(1)} %copy-done.24, f32[64]{0:T(128)S(1)} %copy-done.25, f32[64]{0:T(128)S(1)} %copy-done.26, f32[64]{0:T(128)S(1)} %copy-done.27, f32[64]{0:T(128)S(1)} %copy-done.28, f32[64]{0:T(128)S(1)} %copy-done.29, ...), kind=kLoop, calls=%fused_computation.144 | loop fusion | flops 5308416 | bytes 3934480 | tf_op jit(solution)/shard_map/convert.6
  67.8 3.5 %fusion.45 = bf16[2,48,32,64]{3,2,1,0:T(8,128)(2,1)S(1)} fusion(f32[64]{0:T(128)S(1)} %get-tuple-element.82, f32[64]{0:T(128)S(1)} %get-tuple-element.83, f32[64]{0:T(128)S(1)} %get-tuple-element.84, f32[64]{0:T(128)S(1)} %get-tuple-element.85, f32[64]{0:T(128)S(1)} %get-tuple-element.86, f32[64]{0:T(128)S(1)} %copy-done.18, f32[64]{0:T(128)S(1)} %copy-done.19, ...), kind=kLoop, calls=%fused_computation.126 | loop fusion | flops 5308416 | bytes 3934480 | tf_op jit(solution)/shard_map/convert.7
  71.3 3.3 %fusion.27 = bf16[2,48,32,64]{3,2,1,0:T(8,128)(2,1)S(1)} fusion(f32[64]{0:T(128)S(1)} %get-tuple-element.92, f32[64]{0:T(128)S(1)} %get-tuple-element.93, f32[64]{0:T(128)S(1)} %get-tuple-element.94, f32[64]{0:T(128)S(1)} %get-tuple-element.95, f32[64]{0:T(128)S(1)} %get-tuple-element.96, f32[64]{0:T(128)S(1)} %get-tuple-element.97, ...), kind=kLoop, calls=%fused_computation.108 | loop fusion | flops 5308416 | bytes 3934480 | tf_op jit(solution)/shard_map/convert.8
  74.7 3.4 %fusion = (bf16[3072,256]{1,0:T(8,128)(2,1)}, f32[3072,256]{1,0:T(8,128)}) fusion(bf16[2,48,32,256]{3,2,1,0:T(8,128)(2,1)S(1)} %copy-done.7, bf16[256,256]{1,0:T(8,128)(2,1)S(1)} %copy-done, bf16[3072,64]{1,0:T(8,128)(2,1)S(1)} %bitcast.171, bf16[3072,64]{1,0:T(8,128)(2,1)S(1)} %bitcast.173, bf16[3072,64]{1,0:T(8,128)(2,1)S(1)} %bitcast.175, ...), kind=kOutput, calls=%fused_computation.6 | convolution fusion | flops 414449664 | bytes 7995392 | tf_op jit(solution)/shard_map/dot_general | solution.py:86
  78.0 2.6 %gather_fusion = bf16[256,256]{1,0:T(8,128)(2,1)S(1)} fusion(bf16[3072,256]{1,0:T(8,128)(2,1)} %get-tuple-element.114, s32[1024]{0:T(1024)S(1)} %pad_clamp_fusion), kind=kCustom, calls=%fused_computation | custom fusion | bytes 263168 | tf_op jit(solution)/shard_map/gather | solution.py:122
  80.6 0.9 fusion.75
  81.5 0.9 fusion.76
  82.6 3.8 %scatter_custom_fusion.3 = f32[3072,256]{1,0:T(8,128)} fusion(s32[256]{0:T(256)S(1)} %bitcast.178, f32[256,256]{1,0:T(8,128)S(1)} %fusion.77, f32[]{:T(128)} %constant.101.clone.1), kind=kCustom, calls=%fused_computation.155 | custom fusion | flops 65536 | bytes 3145732 | tf_op jit(solution)/shard_map/scatter-add | solution.py:131
  86.4 4.0 %multiply_convert_fusion = bf16[3072,256]{1,0:T(8,128)(2,1)S(1)} fusion(f32[3072,256]{1,0:T(8,128)} %get-tuple-element.115, f32[3072,256]{1,0:T(8,128)} %scatter_custom_fusion.3), kind=kLoop, calls=%fused_computation.7 | loop fusion | flops 7077888 | bytes 7864320 | tf_op jit(solution)/shard_map/convert_element_type | solution.py:133
  90.5 1.1 copy-done.8
  91.6 2.2 %fusion.91 = f32[256,256]{1,0:T(8,128)} fusion(bf16[3072,256]{1,0:T(8,128)(2,1)S(1)} %multiply_convert_fusion, bf16[3072,64]{1,0:T(8,128)(2,1)S(1)} %bitcast.172, bf16[3072,64]{1,0:T(8,128)(2,1)S(1)} %bitcast.174, bf16[3072,64]{1,0:T(8,128)(2,1)S(1)} %bitcast.176, bf16[3072,64]{1,0:T(8,128)(2,1)S(1)} %bitcast.170), kind=kOutput, calls=%fused_computation.232 | convolution fusion | flops 408944640 | bytes 3407872 | tf_op jit(solution)/shard_map/dot_general | solution.py:134
  93.8 2.1 %fusion.96 = f32[3072,256]{1,0:T(8,128)S(1)} fusion(bf16[3072,256]{1,0:T(8,128)(2,1)} %copy-done.8, bf16[256,256]{1,0:T(8,128)(2,1)S(1)} %copy-done), kind=kOutput, calls=%fused_computation.237 | convolution fusion | flops 402653184 | bytes 4849664 | tf_op jit(solution)/shard_map/dot_general | solution.py:137
  96.0 1.7 copy-done.5
  97.6 10.6 %fusion.18 = (f32[64]{0:T(128)S(1)}, f32[64]{0:T(128)S(1)}, f32[64]{0:T(128)S(1)}, f32[64]{0:T(128)S(1)}, f32[64]{0:T(128)S(1)}, /*index=5*/f32[64]{0:T(128)S(1)...) fusion(f32[2,48,32,256]{3,2,1,0:T(8,128)S(1)} %bitcast.167, ...), kind=kLoop, calls=%fused_computation.99 | loop fusion | flops 14154240 | bytes 11802672 | tf_op jit(solution)/shard_map/reduce_sum | solution.py:66
  108.3 7.1 %fusion.36 = (f32[64]{0:T(128)S(1)}, f32[64]{0:T(128)S(1)}, f32[64]{0:T(128)S(1)}, f32[64]{0:T(128)S(1)}, f32[64]{0:T(128)S(1)}, /*index=5*/f32[64]{0:T(128)S(1)...) fusion(f32[2,48,32,256]{3,2,1,0:T(8,128)} %bitcast.168, ...), kind=kLoop, calls=%fused_computation.117 | loop fusion | flops 7077120 | bytes 7867408 | tf_op jit(solution)/shard_map/reduce_sum | solution.py:66
  115.6 53.6 %all-reduce = (f32[9,256]{1,0:T(8,128)}, f32[]{:T(128)}) all-reduce(f32[9,256]{1,0:T(8,128)S(1)} %pad_maximum_fusion.5, f32[]{:T(128)} %get-tuple-element.116), channel_id=1, replica_groups=mesh['groups'=2,'lon'=8,'lat'=2] {'lon','lat'}, use_global_device_ids=true, to_apply=%region_41.42 | all-reduce | flops 2305 | bytes 18440 | tf_op jit(solution)/shard_map/psum | solution.py:141
  169.9 31.0 %all-reduce.4.cloned.1.call-done = (f32[256,256]{1,0:T(8,128)}, f32[256,227]{0,1:T(8,128)}) async-done(((f32[256,256]{1,0:T(8,128)}, f32[256,227]{0,1:T(8,128)}), (f32[256,256]{1,0:T(8,128)}, f32[256,227]{0,1:T(8,128)})) %all-reduce.4.cloned.1.call-update) | async-done | bytes 494608 | tf_op jit(solution)/shard_map/psum | solution.py:141
  200.8 1.7 copy.23
  202.5 1.6 copy.24
  (87 shorter events, 1.7 us)
Async XLA Ops:
  7.2 67.5 %copy-start = (bf16[256,256]{1,0:T(8,128)(2,1)S(1)}, bf16[256,256]{1,0:T(8,128)(2,1)}, u32[]{:S(2)}) copy-start(bf16[256,256]{1,0:T(8,128)(2,1)} %param.12) | copy-start | bytes 393220
  7.2 45.5 %copy-start.6 = (bf16[2,48,32,256]{3,2,1,0:T(8,128)(2,1)S(1)}, bf16[2,48,32,256]{3,2,1,0:T(8,128)(2,1)}, u32[]{:S(2)}) copy-start(bf16[2,48,32,256]{3,2,1,0:T(8,128)(2,1)} %param.9) | copy-start | bytes 4718596
  10.3 25.5 %all-to-all-start.1 = ((s32[16,2,1]{1,2,0:T(1,128)}), s32[16,2,1]{1,2,0:T(1,128)S(1)}, u32[]{:S(2)}, u32[]{:S(2)}) async-start(s32[16,2,1]{1,2,0:T(1,128)} %bitcast.8), calls=%async_computation.1 | async-start | bytes 16384 | tf_op jit(solution)/shard_map/all_to_all | solution.py:107
  17.8 34.8 %collective-permute-start = (bf16[2,48,4,256]{3,2,1,0:T(4,128)(2,1)S(1)}, bf16[2,48,4,256]{3,2,1,0:T(4,128)(2,1)S(1)}, u32[]{:S(2)}, u32[]{:S(2)}) collective-permute-start(bf16[2,48,4,256]{3,2,1,0:T(4,128)(2,1)S(1)} %get-tuple-element.70), channel_id=1, source_target_pairs={{0,2},{2,4},{4,6},{6,8},{8,10},{10,12},{12,14},{14,0},{1,3},{3,5},... | collective-permute-start | bytes 589832 | tf_op jit(solution)/shard_map/ppermute | solution.py:19
  19.3 33.3 %collective-permute-start.1 = (bf16[2,48,4,256]{3,2,1,0:T(4,128)(2,1)S(1)}, bf16[2,48,4,256]{3,2,1,0:T(4,128)(2,1)S(1)}, u32[]{:S(2)}, u32[]{:S(2)}) collective-permute-start(bf16[2,48,4,256]{3,2,1,0:T(4,128)(2,1)S(1)} %get-tuple-element.71), channel_id=1, source_target_pairs={{2,0},{4,2},{6,4},{8,6},{10,8},{12,10},{14,12},{0,14},{3,1},{5,3},... | collective-permute-start | bytes 589832 | tf_op jit(solution)/shard_map/ppermute | solution.py:21
  35.8 10.2 %all-to-all-start = ((s32[16,2,1]{1,2,0:T(1,128)}), s32[16,2,1]{1,2,0:T(1,128)S(1)}, u32[]{:S(2)}, u32[]{:S(2)}) async-start(s32[16,2,1]{1,2,0:T(1,128)} %bitcast.6), calls=%async_computation | async-start | bytes 16384 | tf_op jit(solution)/shard_map/all_to_all | solution.py:106
  45.9 10.8 %all-to-all-start.2 = ((bf16[32,8,227]{2,1,0:T(8,128)(2,1)}), bf16[32,8,227]{2,1,0:T(8,128)(2,1)S(1)}, u32[]{:S(2)}, u32[]{:S(2)}) async-start(bf16[32,8,227]{2,1,0:T(8,128)(2,1)} %scatter_fusion), calls=%async_computation.2 | async-start | bytes 262144 | tf_op jit(solution)/shard_map/all_to_all | solution.py:105
  51.3 149.5 %all-reduce.4.cloned.1.call-start = ((), (), s32[]{:S(2)}) async-start(), calls=%async_computation.3 | async-start | bytes 999424 | tf_op jit(solution)/shard_map/psum | solution.py:141
  52.8 4.1 %collective-permute-start.2 = (bf16[2,4,40,256]{3,2,1,0:T(8,128)(2,1)S(1)}, bf16[2,4,40,256]{3,2,1,0:T(8,128)(2,1)S(1)}, u32[]{:S(2)}, u32[]{:S(2)}) collective-permute-start(bf16[2,4,40,256]{3,2,1,0:T(8,128)(2,1)S(1)} %get-tuple-element.68), channel_id=1, source_target_pairs={{0,1},{2,3},{4,5},{6,7},{8,9},{10,11},{12,13},{14,15},{16,17},{18,... | collective-permute-start | bytes 491528 | tf_op jit(solution)/shard_map/ppermute | solution.py:19
  54.9 3.3 %collective-permute-start.3 = (bf16[2,4,40,256]{3,2,1,0:T(8,128)(2,1)S(1)}, bf16[2,4,40,256]{3,2,1,0:T(8,128)(2,1)S(1)}, u32[]{:S(2)}, u32[]{:S(2)}) collective-permute-start(bf16[2,4,40,256]{3,2,1,0:T(8,128)(2,1)S(1)} %get-tuple-element.69), channel_id=1, source_target_pairs={{1,0},{3,2},{5,4},{7,6},{9,8},{11,10},{13,12},{15,14},{17,16},{19,... | collective-permute-start | bytes 491528 | tf_op jit(solution)/shard_map/ppermute | solution.py:21
  59.6 1.4 copy-start.7
  59.6 1.4 copy-start.31
  60.6 3.9 %copy-start.1 = (bf16[2,56,40,64]{3,2,1,0:T(8,128)(2,1)}, bf16[2,56,40,64]{3,2,1,0:T(8,128)(2,1)S(1)}, u32[]{:S(2)}) copy-start(bf16[2,56,40,64]{3,2,1,0:T(8,128)(2,1)S(1)} %get-tuple-element.65) | copy-start | bytes 1720324
  60.6 7.1 %copy-start.3 = (bf16[2,56,40,64]{3,2,1,0:T(8,128)(2,1)}, bf16[2,56,40,64]{3,2,1,0:T(8,128)(2,1)S(1)}, u32[]{:S(2)}) copy-start(bf16[2,56,40,64]{3,2,1,0:T(8,128)(2,1)S(1)} %get-tuple-element.66) | copy-start | bytes 1720324
  61.0 3.6 %copy-start.22 = (f32[64]{0:T(128)S(1)}, f32[64]{0:T(128)}, u32[]{:S(2)}) copy-start(f32[64]{0:T(128)} %get-tuple-element.73) | copy-start | bytes 772
  61.0 3.6 %copy-start.23 = (f32[64]{0:T(128)S(1)}, f32[64]{0:T(128)}, u32[]{:S(2)}) copy-start(f32[64]{0:T(128)} %get-tuple-element.74) | copy-start | bytes 772
  61.0 3.6 %copy-start.24 = (f32[64]{0:T(128)S(1)}, f32[64]{0:T(128)}, u32[]{:S(2)}) copy-start(f32[64]{0:T(128)} %get-tuple-element.75) | copy-start | bytes 772
  61.0 3.6 %copy-start.25 = (f32[64]{0:T(128)S(1)}, f32[64]{0:T(128)}, u32[]{:S(2)}) copy-start(f32[64]{0:T(128)} %get-tuple-element.76) | copy-start | bytes 772
  61.0 3.6 %copy-start.26 = (f32[64]{0:T(128)S(1)}, f32[64]{0:T(128)}, u32[]{:S(2)}) copy-start(f32[64]{0:T(128)} %get-tuple-element.77) | copy-start | bytes 772
  61.0 3.6 %copy-start.27 = (f32[64]{0:T(128)S(1)}, f32[64]{0:T(128)}, u32[]{:S(2)}) copy-start(f32[64]{0:T(128)} %get-tuple-element.78) | copy-start | bytes 772
  61.0 3.6 %copy-start.28 = (f32[64]{0:T(128)S(1)}, f32[64]{0:T(128)}, u32[]{:S(2)}) copy-start(f32[64]{0:T(128)} %get-tuple-element.79) | copy-start | bytes 772
  61.0 3.6 %copy-start.29 = (f32[64]{0:T(128)S(1)}, f32[64]{0:T(128)}, u32[]{:S(2)}) copy-start(f32[64]{0:T(128)} %get-tuple-element.80) | copy-start | bytes 772
  61.0 3.6 %copy-start.30 = (f32[64]{0:T(128)S(1)}, f32[64]{0:T(128)}, u32[]{:S(2)}) copy-start(f32[64]{0:T(128)} %get-tuple-element.81) | copy-start | bytes 772
  64.5 10.1 %copy-start.9 = (bf16[2,48,32,64]{3,2,1,0:T(8,128)(2,1)}, bf16[2,48,32,64]{3,2,1,0:T(8,128)(2,1)S(1)}, u32[]{:S(2)}) copy-start(bf16[2,48,32,64]{3,2,1,0:T(8,128)(2,1)S(1)} %fusion.9) | copy-start | bytes 1179652
  64.6 3.2 %copy-start.18 = (f32[64]{0:T(128)S(1)}, f32[64]{0:T(128)}, u32[]{:S(2)}) copy-start(f32[64]{0:T(128)} %get-tuple-element.87) | copy-start | bytes 772
  64.6 3.2 %copy-start.19 = (f32[64]{0:T(128)S(1)}, f32[64]{0:T(128)}, u32[]{:S(2)}) copy-start(f32[64]{0:T(128)} %get-tuple-element.88) | copy-start | bytes 772
  64.6 3.2 %copy-start.20 = (f32[64]{0:T(128)S(1)}, f32[64]{0:T(128)}, u32[]{:S(2)}) copy-start(f32[64]{0:T(128)} %get-tuple-element.89) | copy-start | bytes 772
  64.6 3.2 %copy-start.21 = (f32[64]{0:T(128)S(1)}, f32[64]{0:T(128)}, u32[]{:S(2)}) copy-start(f32[64]{0:T(128)} %get-tuple-element.90) | copy-start | bytes 772
  67.7 6.9 %copy-start.11 = (bf16[2,48,32,64]{3,2,1,0:T(8,128)(2,1)}, bf16[2,48,32,64]{3,2,1,0:T(8,128)(2,1)S(1)}, u32[]{:S(2)}) copy-start(bf16[2,48,32,64]{3,2,1,0:T(8,128)(2,1)S(1)} %fusion.63) | copy-start | bytes 1179652
  71.3 3.4 %copy-start.13 = (bf16[2,48,32,64]{3,2,1,0:T(8,128)(2,1)}, bf16[2,48,32,64]{3,2,1,0:T(8,128)(2,1)S(1)}, u32[]{:S(2)}) copy-start(bf16[2,48,32,64]{3,2,1,0:T(8,128)(2,1)S(1)} %fusion.45) | copy-start | bytes 1179652
  74.6 3.4 %copy-start.15 = (bf16[2,48,32,64]{3,2,1,0:T(8,128)(2,1)}, bf16[2,48,32,64]{3,2,1,0:T(8,128)(2,1)S(1)}, u32[]{:S(2)}) copy-start(bf16[2,48,32,64]{3,2,1,0:T(8,128)(2,1)S(1)} %fusion.27) | copy-start | bytes 1179652
  74.6 6.0 %copy-start.17 = (bf16[256,227]{0,1:T(8,128)(2,1)S(1)}, bf16[256,227]{0,1:T(8,128)(2,1)}, u32[]{:S(2)}) copy-start(bf16[256,227]{0,1:T(8,128)(2,1)} %param.13) | copy-start | bytes 348676
  86.4 5.2 %copy-start.10 = (bf16[2,48,32,64]{3,2,1,0:T(8,128)(2,1)S(1)}, bf16[2,48,32,64]{3,2,1,0:T(8,128)(2,1)}, u32[]{:S(2)}) copy-start(bf16[2,48,32,64]{3,2,1,0:T(8,128)(2,1)} %copy-done.9) | copy-start | bytes 1179652
  86.4 5.2 %copy-start.12 = (bf16[2,48,32,64]{3,2,1,0:T(8,128)(2,1)S(1)}, bf16[2,48,32,64]{3,2,1,0:T(8,128)(2,1)}, u32[]{:S(2)}) copy-start(bf16[2,48,32,64]{3,2,1,0:T(8,128)(2,1)} %copy-done.11) | copy-start | bytes 1179652
  86.4 5.2 %copy-start.14 = (bf16[2,48,32,64]{3,2,1,0:T(8,128)(2,1)S(1)}, bf16[2,48,32,64]{3,2,1,0:T(8,128)(2,1)}, u32[]{:S(2)}) copy-start(bf16[2,48,32,64]{3,2,1,0:T(8,128)(2,1)} %copy-done.13) | copy-start | bytes 1179652
  86.4 5.2 %copy-start.16 = (bf16[2,48,32,64]{3,2,1,0:T(8,128)(2,1)S(1)}, bf16[2,48,32,64]{3,2,1,0:T(8,128)(2,1)}, u32[]{:S(2)}) copy-start(bf16[2,48,32,64]{3,2,1,0:T(8,128)(2,1)} %copy-done.15) | copy-start | bytes 1179652
  90.5 1.2 copy-start.8
  93.8 3.8 %copy-start.2 = (bf16[2,56,40,64]{3,2,1,0:T(8,128)(2,1)S(1)}, bf16[2,56,40,64]{3,2,1,0:T(8,128)(2,1)}, u32[]{:S(2)}) copy-start(bf16[2,56,40,64]{3,2,1,0:T(8,128)(2,1)} %copy-done.1) | copy-start | bytes 1720324
  93.8 3.8 %copy-start.4 = (bf16[2,56,40,64]{3,2,1,0:T(8,128)(2,1)S(1)}, bf16[2,56,40,64]{3,2,1,0:T(8,128)(2,1)}, u32[]{:S(2)}) copy-start(bf16[2,56,40,64]{3,2,1,0:T(8,128)(2,1)} %copy-done.3) | copy-start | bytes 1720324
  96.0 1.7 copy-start.5
Sparse Core Ops, SparseCore 0:
  108.4 92.4 all-reduce.3
where the time goes:
time: 213 us; the launch traced here: 212 us
  blocking collectives  53.6 us (25%)
  other arithmetic  44.3 us (21%)
  waiting for transfers between devices  33.5 us (16%)
  between operations  27 us (13%)
  starting transfers between devices  23.2 us (11%)
  local copies, waits for them, and re-layouts  20.8 us (10%)
  matrix products  9.67 us (5%)
    psum x1, blocking collectives, local(): lax.psum((grad_dw, grad_pw, grad_head, loss_sum), ('lon', 'lat'))  53.6 us
    psum x1, waiting for transfers between devices, local(): lax.psum((grad_dw, grad_pw, grad_head, loss_sum), ('lon', 'lat'))  31 us
    reduce_sum x2, other arithmetic, dilated_grad(): jnp.sum((window.astype(jnp.float32) * group_grad).reshape(-1, group_width...  17.7 us
    another operation x4, other arithmetic  13.3 us
    unnamed x66, local copies, waits for them, and re-layouts  6.59 us
    all_to_all x1, starting transfers between devices, local(): lax.all_to_all(send_count, ('lon', 'lat'), split_axis=0, concat_axis=0, t...  6.27 us
    all_to_all x1, starting transfers between devices, local(): lax.all_to_all(send_tiles, ('lon', 'lat'), split_axis=0, concat_axis=0, t...  5.39 us
    all_to_all x1, starting transfers between devices, local(): lax.all_to_all(send_start, ('lon', 'lat'), split_axis=0, concat_axis=0, t...  5.18 us
  transfers between devices with their start and end apart: 8, of which 4 were waited for; matrix products, arithmetic and copies ran while one was open for 9% of the time, Pallas kernels for 0%

commit v1 on v0

--- a/solution.py
+++ b/solution.py
@@ -6,6 +6,11 @@
 DMAX = 4
 TILE = 8
 CAP = 2
+
+
+def axis_by_axis(value, axis_one, axis_two):
+    partial = lax.psum(value, axis_one)
+    return lax.psum(partial, axis_two)
 
 
 def padded_2(cells, sides, width, closed):
@@ -138,8 +143,8 @@
         micro_batch, band_rows, block_cols, width
     )
     grad_dw = dilated_grad(padded, grad_z, rates, band_rows, block_cols)
-    grad_dw, grad_pw, grad_head, loss_sum = lax.psum(
-        (grad_dw, grad_pw, grad_head, loss_sum), ("lon", "lat")
+    grad_dw, grad_pw, grad_head, loss_sum = axis_by_axis(
+        (grad_dw, grad_pw, grad_head, loss_sum), "lat", "lon"
     )
     return (grad_dw, grad_pw, grad_head, (loss_sum / teach_width).reshape(1))
 

time: 213 us -> 208 us (0.977)
  blocking collectives: 53.6 us -> 39.6 us
  other arithmetic: 44.3 us -> 52.3 us
    psum x1 -> x2, blocking collectives: 53.6 us -> 39.6 us  [the longest x1 35 us: axis_by_axis(): return lax.psum(partial, axis_two)]
    reduce_sum x2, other arithmetic: 17.7 us -> 25.6 us  [dilated_grad(): jnp.sum((window.astype(jnp.float32) * group_grad).reshape(-1, group_width...]
    unnamed x66 -> x60, local copies, waits for them, and re-layouts: 6.59 us -> 4.91 us
    psum x1 -> x2, waiting for transfers between devices: 31 us -> 30.5 us  [the longest x1 29 us: axis_by_axis(): return lax.psum(partial, axis_two)]
  transfers between devices with their start and end apart: 8 -> 9, of which waited for: 4 -> 5; matrix products, arithmetic and copies ran while one was open for 9% -> 18% of each run, Pallas kernels for 0% -> 0%
where the time goes in v1:
time: 208 us; the launch traced here: 205 us
  other arithmetic  52.3 us (25%)
  blocking collectives  39.6 us (19%)
  waiting for transfers between devices  33 us (16%)
  between operations  27 us (13%)
  starting transfers between devices  23.3 us (11%)
  local copies, waits for them, and re-layouts  19.1 us (9%)
  matrix products  11.2 us (5%)
    psum x1, blocking collectives, axis_by_axis(): return lax.psum(partial, axis_two)  35 us
    psum x1, waiting for transfers between devices, axis_by_axis(): return lax.psum(partial, axis_two)  29 us
    reduce_sum x2, other arithmetic, dilated_grad(): jnp.sum((window.astype(jnp.float32) * group_grad).reshape(-1, group_width...  25.6 us
    another operation x4, other arithmetic  13.3 us
    all_to_all x1, starting transfers between devices, local(): lax.all_to_all(send_count, ('lon', 'lat'), split_axis=0, concat_axis=0, t...  6.27 us
    all_to_all x1, starting transfers between devices, local(): lax.all_to_all(send_tiles, ('lon', 'lat'), split_axis=0, concat_axis=0, t...  5.39 us
    all_to_all x1, starting transfers between devices, local(): lax.all_to_all(send_start, ('lon', 'lat'), split_axis=0, concat_axis=0, t...  5.18 us
    unnamed x60, local copies, waits for them, and re-layouts  4.91 us
  transfers between devices with their start and end apart: 9, of which 5 were waited for; matrix products, arithmetic and copies ran while one was open for 18% of the time, Pallas kernels for 0%

profile of v1, /device:TPU:8, one launch (start us, length us, event | category | flops | bytes accessed | tf_op | source)
XLA Modules:
  0.0 205.4 jit_solution(5340201135564278929)
XLA Ops:
  7.2 1.0 convert_reduce_fusion
  8.2 0.7 fusion.86
  8.8 0.8 scatter_custom_fusion.1
  9.6 0.7 all_to_all.17
  10.3 6.3 %all-to-all-start.1 = ((s32[16,2,1]{1,2,0:T(1,128)}), s32[16,2,1]{1,2,0:T(1,128)S(1)}, u32[]{:S(2)}, u32[]{:S(2)}) async-start(s32[16,2,1]{1,2,0:T(1,128)} %bitcast.8), calls=%async_computation.1 | async-start | bytes 16384 | tf_op jit(solution)/shard_map/all_to_all | solution.py:112
  16.5 1.3 fusion.94
  17.8 1.5 collective-permute-start
  19.3 1.5 collective-permute-start.1
  20.8 1.4 fusion.95
  32.8 0.7 convert_element_type.185
  33.5 0.7 slice_bitcast_fusion.35
  34.2 0.8 scatter_custom_fusion
  35.1 0.7 all_to_all.15
  35.8 5.2 %all-to-all-start = ((s32[16,2,1]{1,2,0:T(1,128)}), s32[16,2,1]{1,2,0:T(1,128)S(1)}, u32[]{:S(2)}, u32[]{:S(2)}) async-start(s32[16,2,1]{1,2,0:T(1,128)} %bitcast.6), calls=%async_computation | async-start | bytes 16384 | tf_op jit(solution)/shard_map/all_to_all | solution.py:111
  41.0 0.7 broadcast_in_dim.15
  41.6 2.3 %scatter_fusion = bf16[32,8,227]{2,1,0:T(8,128)(2,1)} fusion(bf16[32,8,227]{2,1,0:T(8,128)(2,1)} %broadcast_in_dim.15, s32[16]{0:T(128)S(1)} %fusion.86, bf16[16,8,227]{2,1,0:T(8,128)(2,1)} %param.14), kind=kCustom, calls=%fused_computation.3 | custom fusion | bytes 174400 | tf_op jit(solution)/shard_map/scatter | solution.py:105
  43.9 0.6 broadcast.181
  44.5 0.6 reduce.43
  45.2 0.7 all-to-all-done
  45.9 5.4 %all-to-all-start.2 = ((bf16[32,8,227]{2,1,0:T(8,128)(2,1)}), bf16[32,8,227]{2,1,0:T(8,128)(2,1)S(1)}, u32[]{:S(2)}, u32[]{:S(2)}) async-start(bf16[32,8,227]{2,1,0:T(8,128)(2,1)} %scatter_fusion), calls=%async_computation.2 | async-start | bytes 262144 | tf_op jit(solution)/shard_map/all_to_all | solution.py:110
  51.4 0.6 reduce.42
  52.8 2.1 %collective-permute-start.2 = (bf16[2,4,40,256]{3,2,1,0:T(8,128)(2,1)S(1)}, bf16[2,4,40,256]{3,2,1,0:T(8,128)(2,1)S(1)}, u32[]{:S(2)}, u32[]{:S(2)}) collective-permute-start(bf16[2,4,40,256]{3,2,1,0:T(8,128)(2,1)S(1)} %get-tuple-element.72), channel_id=1, source_target_pairs={{0,1},{2,3},{4,5},{6,7},{8,9},{10,11},{12,13},{14,15},{16,17},{18,... | collective-permute-start | bytes 491528 | tf_op jit(solution)/shard_map/ppermute | solution.py:24
  54.9 1.3 collective-permute-start.3
  56.2 0.5 all-to-all-done.2
  56.9 1.3 collective-permute-done.3
  58.2 1.4 pad_maximum_fusion
  59.6 1.0 fusion.93
  61.0 3.5 %fusion.9 = bf16[2,48,32,64]{3,2,1,0:T(8,128)(2,1)S(1)} fusion(f32[64]{0:T(128)S(1)} %get-tuple-element.105, f32[64]{0:T(128)S(1)} %get-tuple-element.106, f32[64]{0:T(128)S(1)} %get-tuple-element.107, f32[64]{0:T(128)S(1)} %get-tuple-element.108, f32[64]{0:T(128)S(1)} %get-tuple-element.109, f32[64]{0:T(128)S(1)} %get-tuple-element.110, ...), kind=kLoop, calls=%fused_computation.90 | loop fusion | flops 5308416 | bytes 3934480 | tf_op jit(solution)/shard_map/convert.9
  64.6 3.1 %fusion.63 = bf16[2,48,32,64]{3,2,1,0:T(8,128)(2,1)S(1)} fusion(f32[64]{0:T(128)S(1)} %copy-done.19, f32[64]{0:T(128)S(1)} %copy-done.20, f32[64]{0:T(128)S(1)} %copy-done.21, f32[64]{0:T(128)S(1)} %copy-done.22, f32[64]{0:T(128)S(1)} %copy-done.23, f32[64]{0:T(128)S(1)} %copy-done.24, f32[64]{0:T(128)S(1)} %copy-done.25, f32[64]{0:T(128)S(1)} %copy-done.26, ...), kind=kLoop, calls=%fused_computation.144 | loop fusion | flops 5308416 | bytes 3934480 | tf_op jit(solution)/shard_map/convert.6
  67.8 3.5 %fusion.45 = bf16[2,48,32,64]{3,2,1,0:T(8,128)(2,1)S(1)} fusion(f32[64]{0:T(128)S(1)} %get-tuple-element.86, f32[64]{0:T(128)S(1)} %get-tuple-element.87, f32[64]{0:T(128)S(1)} %get-tuple-element.88, f32[64]{0:T(128)S(1)} %get-tuple-element.89, f32[64]{0:T(128)S(1)} %get-tuple-element.90, f32[64]{0:T(128)S(1)} %copy-done.15, f32[64]{0:T(128)S(1)} %copy-done.16, ...), kind=kLoop, calls=%fused_computation.126 | loop fusion | flops 5308416 | bytes 3934480 | tf_op jit(solution)/shard_map/convert.7
  71.3 3.3 %fusion.27 = bf16[2,48,32,64]{3,2,1,0:T(8,128)(2,1)S(1)} fusion(f32[64]{0:T(128)S(1)} %get-tuple-element.96, f32[64]{0:T(128)S(1)} %get-tuple-element.97, f32[64]{0:T(128)S(1)} %get-tuple-element.98, f32[64]{0:T(128)S(1)} %get-tuple-element.99, f32[64]{0:T(128)S(1)} %get-tuple-element.100, f32[64]{0:T(128)S(1)} %get-tuple-element.101, ...), kind=kLoop, calls=%fused_computation.108 | loop fusion | flops 5308416 | bytes 3934480 | tf_op jit(solution)/shard_map/convert.8
  74.7 3.4 %fusion = (bf16[3072,256]{1,0:T(8,128)(2,1)}, f32[3072,256]{1,0:T(8,128)}) fusion(bf16[2,48,32,256]{3,2,1,0:T(8,128)(2,1)S(1)} %copy-done.4, bf16[256,256]{1,0:T(8,128)(2,1)S(1)} %copy-done, bf16[3072,64]{1,0:T(8,128)(2,1)S(1)} %bitcast.171, bf16[3072,64]{1,0:T(8,128)(2,1)S(1)} %bitcast.173, bf16[3072,64]{1,0:T(8,128)(2,1)S(1)} %bitcast.175, ...), kind=kOutput, calls=%fused_computation.6 | convolution fusion | flops 414449664 | bytes 7995392 | tf_op jit(solution)/shard_map/dot_general | solution.py:91
  78.0 2.6 %gather_fusion = bf16[256,256]{1,0:T(8,128)(2,1)S(1)} fusion(bf16[3072,256]{1,0:T(8,128)(2,1)} %get-tuple-element.118, s32[1024]{0:T(1024)S(1)} %pad_clamp_fusion), kind=kCustom, calls=%fused_computation | custom fusion | bytes 263168 | tf_op jit(solution)/shard_map/gather | solution.py:127
  80.6 0.9 fusion.75
  81.5 0.9 fusion.76
  82.6 3.8 %scatter_custom_fusion.3 = f32[3072,256]{1,0:T(8,128)} fusion(s32[256]{0:T(256)S(1)} %bitcast.178, f32[256,256]{1,0:T(8,128)S(1)} %fusion.77, f32[]{:T(128)} %constant.101.clone.1), kind=kCustom, calls=%fused_computation.155 | custom fusion | flops 65536 | bytes 3145732 | tf_op jit(solution)/shard_map/scatter-add | solution.py:136
  86.4 4.0 %multiply_convert_fusion = bf16[3072,256]{1,0:T(8,128)(2,1)S(1)} fusion(f32[3072,256]{1,0:T(8,128)} %get-tuple-element.119, f32[3072,256]{1,0:T(8,128)} %scatter_custom_fusion.3), kind=kLoop, calls=%fused_computation.7 | loop fusion | flops 7077888 | bytes 7864320 | tf_op jit(solution)/shard_map/convert_element_type | solution.py:138
  90.5 1.1 copy-done.5
  91.6 2.2 %fusion.91 = f32[256,256]{1,0:T(8,128)} fusion(bf16[3072,256]{1,0:T(8,128)(2,1)S(1)} %multiply_convert_fusion, bf16[3072,64]{1,0:T(8,128)(2,1)S(1)} %bitcast.172, bf16[3072,64]{1,0:T(8,128)(2,1)S(1)} %bitcast.174, bf16[3072,64]{1,0:T(8,128)(2,1)S(1)} %bitcast.176, bf16[3072,64]{1,0:T(8,128)(2,1)S(1)} %bitcast.170), kind=kOutput, calls=%fused_computation.232 | convolution fusion | flops 408944640 | bytes 3407872 | tf_op jit(solution)/shard_map/dot_general | solution.py:139
  93.8 3.7 %fusion.96 = f32[3072,256]{1,0:T(8,128)} fusion(bf16[3072,256]{1,0:T(8,128)(2,1)} %copy-done.5, bf16[256,256]{1,0:T(8,128)(2,1)S(1)} %copy-done), kind=kOutput, calls=%fused_computation.237 | convolution fusion | flops 402653184 | bytes 4849664 | tf_op jit(solution)/shard_map/dot_general | solution.py:142
  97.5 18.5 %fusion.18 = (f32[64]{0:T(128)S(1)}, f32[64]{0:T(128)S(1)}, f32[64]{0:T(128)S(1)}, f32[64]{0:T(128)S(1)}, f32[64]{0:T(128)S(1)}, /*index=5*/f32[64]{0:T(128)S(1)...) fusion(f32[2,48,32,256]{3,2,1,0:T(8,128)} %bitcast.167, ...), kind=kLoop, calls=%fused_computation.99 | loop fusion | flops 14154240 | bytes 11802672 | tf_op jit(solution)/shard_map/reduce_sum | solution.py:71
  116.1 1.5 all-reduce.9.cloned.1.call-done
  117.6 7.1 %fusion.36 = (f32[64]{0:T(128)S(1)}, f32[64]{0:T(128)S(1)}, f32[64]{0:T(128)S(1)}, f32[64]{0:T(128)S(1)}, f32[64]{0:T(128)S(1)}, /*index=5*/f32[64]{0:T(128)S(1)...) fusion(f32[2,48,32,256]{3,2,1,0:T(8,128)} %bitcast.168, ...), kind=kLoop, calls=%fused_computation.117 | loop fusion | flops 7077120 | bytes 7867408 | tf_op jit(solution)/shard_map/reduce_sum | solution.py:71
  124.9 4.6 %all-reduce.2 = (f32[9,256]{1,0:T(8,128)S(1)}, f32[]{:T(128)}) all-reduce(f32[9,256]{1,0:T(8,128)S(1)} %pad_maximum_fusion.5, f32[]{:T(128)} %get-tuple-element.120), channel_id=1, replica_groups=mesh['groups'=2,'lon'=8,'lat'=2] {'lat'}, use_global_device_ids=true, to_apply=%region_41.42 | all-reduce | flops 2305 | bytes 18440 | tf_op jit(solution)/shard_map/psum | solution.py:12
  129.5 35.0 %all-reduce = (f32[9,256]{1,0:T(8,128)}, f32[]{:T(128)}) all-reduce(f32[9,256]{1,0:T(8,128)S(1)} %get-tuple-element.44, f32[]{:T(128)} %get-tuple-element.45), channel_id=1, replica_groups=mesh['groups'=2,'lon'=8,'lat'=2] {'lon'}, use_global_device_ids=true, to_apply=%region_42.43 | all-reduce | flops 2305 | bytes 18440 | tf_op jit(solution)/shard_map/psum | solution.py:13
  165.1 29.0 %all-reduce.7.cloned.1.call-done = (f32[256,256]{1,0:T(8,128)}, f32[256,227]{0,1:T(8,128)}) async-done(((f32[256,256]{1,0:T(8,128)}, f32[256,227]{0,1:T(8,128)}), (f32[256,256]{1,0:T(8,128)}, f32[256,227]{0,1:T(8,128)})) %all-reduce.7.cloned.1.call-update) | async-done | bytes 494608 | tf_op jit(solution)/shard_map/psum | solution.py:13
  194.1 1.7 copy.25
  195.8 1.6 copy.26
  (85 shorter events, 2.1 us)
Async XLA Ops:
  7.2 67.5 %copy-start = (bf16[256,256]{1,0:T(8,128)(2,1)S(1)}, bf16[256,256]{1,0:T(8,128)(2,1)}, u32[]{:S(2)}) copy-start(bf16[256,256]{1,0:T(8,128)(2,1)} %param.12) | copy-start | bytes 393220
  7.2 45.5 %copy-start.3 = (bf16[2,48,32,256]{3,2,1,0:T(8,128)(2,1)S(1)}, bf16[2,48,32,256]{3,2,1,0:T(8,128)(2,1)}, u32[]{:S(2)}) copy-start(bf16[2,48,32,256]{3,2,1,0:T(8,128)(2,1)} %param.9) | copy-start | bytes 4718596
  10.3 25.5 %all-to-all-start.1 = ((s32[16,2,1]{1,2,0:T(1,128)}), s32[16,2,1]{1,2,0:T(1,128)S(1)}, u32[]{:S(2)}, u32[]{:S(2)}) async-start(s32[16,2,1]{1,2,0:T(1,128)} %bitcast.8), calls=%async_computation.1 | async-start | bytes 16384 | tf_op jit(solution)/shard_map/all_to_all | solution.py:112
  17.8 34.8 %collective-permute-start = (bf16[2,48,4,256]{3,2,1,0:T(4,128)(2,1)S(1)}, bf16[2,48,4,256]{3,2,1,0:T(4,128)(2,1)S(1)}, u32[]{:S(2)}, u32[]{:S(2)}) collective-permute-start(bf16[2,48,4,256]{3,2,1,0:T(4,128)(2,1)S(1)} %get-tuple-element.74), channel_id=1, source_target_pairs={{0,2},{2,4},{4,6},{6,8},{8,10},{10,12},{12,14},{14,0},{1,3},{3,5},... | collective-permute-start | bytes 589832 | tf_op jit(solution)/shard_map/ppermute | solution.py:24
  19.3 33.3 %collective-permute-start.1 = (bf16[2,48,4,256]{3,2,1,0:T(4,128)(2,1)S(1)}, bf16[2,48,4,256]{3,2,1,0:T(4,128)(2,1)S(1)}, u32[]{:S(2)}, u32[]{:S(2)}) collective-permute-start(bf16[2,48,4,256]{3,2,1,0:T(4,128)(2,1)S(1)} %get-tuple-element.75), channel_id=1, source_target_pairs={{2,0},{4,2},{6,4},{8,6},{10,8},{12,10},{14,12},{0,14},{3,1},{5,3},... | collective-permute-start | bytes 589832 | tf_op jit(solution)/shard_map/ppermute | solution.py:26
  35.8 10.2 %all-to-all-start = ((s32[16,2,1]{1,2,0:T(1,128)}), s32[16,2,1]{1,2,0:T(1,128)S(1)}, u32[]{:S(2)}, u32[]{:S(2)}) async-start(s32[16,2,1]{1,2,0:T(1,128)} %bitcast.6), calls=%async_computation | async-start | bytes 16384 | tf_op jit(solution)/shard_map/all_to_all | solution.py:111
  45.9 10.8 %all-to-all-start.2 = ((bf16[32,8,227]{2,1,0:T(8,128)(2,1)}), bf16[32,8,227]{2,1,0:T(8,128)(2,1)S(1)}, u32[]{:S(2)}, u32[]{:S(2)}) async-start(bf16[32,8,227]{2,1,0:T(8,128)(2,1)} %scatter_fusion), calls=%async_computation.2 | async-start | bytes 262144 | tf_op jit(solution)/shard_map/all_to_all | solution.py:110
  51.3 66.2 %all-reduce.9.cloned.1.call-start = ((), (), s32[]{:S(2)}) async-start(), calls=%async_computation.4 | async-start | bytes 999424 | tf_op jit(solution)/shard_map/psum | solution.py:12
  52.8 4.1 %collective-permute-start.2 = (bf16[2,4,40,256]{3,2,1,0:T(8,128)(2,1)S(1)}, bf16[2,4,40,256]{3,2,1,0:T(8,128)(2,1)S(1)}, u32[]{:S(2)}, u32[]{:S(2)}) collective-permute-start(bf16[2,4,40,256]{3,2,1,0:T(8,128)(2,1)S(1)} %get-tuple-element.72), channel_id=1, source_target_pairs={{0,1},{2,3},{4,5},{6,7},{8,9},{10,11},{12,13},{14,15},{16,17},{18,... | collective-permute-start | bytes 491528 | tf_op jit(solution)/shard_map/ppermute | solution.py:24
  54.9 3.3 %collective-permute-start.3 = (bf16[2,4,40,256]{3,2,1,0:T(8,128)(2,1)S(1)}, bf16[2,4,40,256]{3,2,1,0:T(8,128)(2,1)S(1)}, u32[]{:S(2)}, u32[]{:S(2)}) collective-permute-start(bf16[2,4,40,256]{3,2,1,0:T(8,128)(2,1)S(1)} %get-tuple-element.73), channel_id=1, source_target_pairs={{1,0},{3,2},{5,4},{7,6},{9,8},{11,10},{13,12},{15,14},{17,16},{19,... | collective-permute-start | bytes 491528 | tf_op jit(solution)/shard_map/ppermute | solution.py:26
  59.6 1.4 copy-start.4
  59.6 1.4 copy-start.28
  60.6 3.9 %copy-start.1 = (bf16[2,56,40,64]{3,2,1,0:T(8,128)(2,1)}, bf16[2,56,40,64]{3,2,1,0:T(8,128)(2,1)S(1)}, u32[]{:S(2)}) copy-start(bf16[2,56,40,64]{3,2,1,0:T(8,128)(2,1)S(1)} %get-tuple-element.69) | copy-start | bytes 1720324
  60.6 7.1 %copy-start.2 = (bf16[2,56,40,64]{3,2,1,0:T(8,128)(2,1)}, bf16[2,56,40,64]{3,2,1,0:T(8,128)(2,1)S(1)}, u32[]{:S(2)}) copy-start(bf16[2,56,40,64]{3,2,1,0:T(8,128)(2,1)S(1)} %get-tuple-element.70) | copy-start | bytes 1720324
  61.0 3.6 %copy-start.19 = (f32[64]{0:T(128)S(1)}, f32[64]{0:T(128)}, u32[]{:S(2)}) copy-start(f32[64]{0:T(128)} %get-tuple-element.77) | copy-start | bytes 772
  61.0 3.6 %copy-start.20 = (f32[64]{0:T(128)S(1)}, f32[64]{0:T(128)}, u32[]{:S(2)}) copy-start(f32[64]{0:T(128)} %get-tuple-element.78) | copy-start | bytes 772
  61.0 3.6 %copy-start.21 = (f32[64]{0:T(128)S(1)}, f32[64]{0:T(128)}, u32[]{:S(2)}) copy-start(f32[64]{0:T(128)} %get-tuple-element.79) | copy-start | bytes 772
  61.0 3.6 %copy-start.22 = (f32[64]{0:T(128)S(1)}, f32[64]{0:T(128)}, u32[]{:S(2)}) copy-start(f32[64]{0:T(128)} %get-tuple-element.80) | copy-start | bytes 772
  61.0 3.6 %copy-start.23 = (f32[64]{0:T(128)S(1)}, f32[64]{0:T(128)}, u32[]{:S(2)}) copy-start(f32[64]{0:T(128)} %get-tuple-element.81) | copy-start | bytes 772
  61.0 3.6 %copy-start.24 = (f32[64]{0:T(128)S(1)}, f32[64]{0:T(128)}, u32[]{:S(2)}) copy-start(f32[64]{0:T(128)} %get-tuple-element.82) | copy-start | bytes 772
  61.0 3.6 %copy-start.25 = (f32[64]{0:T(128)S(1)}, f32[64]{0:T(128)}, u32[]{:S(2)}) copy-start(f32[64]{0:T(128)} %get-tuple-element.83) | copy-start | bytes 772
  61.0 3.6 %copy-start.26 = (f32[64]{0:T(128)S(1)}, f32[64]{0:T(128)}, u32[]{:S(2)}) copy-start(f32[64]{0:T(128)} %get-tuple-element.84) | copy-start | bytes 772
  61.0 3.6 %copy-start.27 = (f32[64]{0:T(128)S(1)}, f32[64]{0:T(128)}, u32[]{:S(2)}) copy-start(f32[64]{0:T(128)} %get-tuple-element.85) | copy-start | bytes 772
  64.5 10.1 %copy-start.6 = (bf16[2,48,32,64]{3,2,1,0:T(8,128)(2,1)}, bf16[2,48,32,64]{3,2,1,0:T(8,128)(2,1)S(1)}, u32[]{:S(2)}) copy-start(bf16[2,48,32,64]{3,2,1,0:T(8,128)(2,1)S(1)} %fusion.9) | copy-start | bytes 1179652
  64.6 3.2 %copy-start.15 = (f32[64]{0:T(128)S(1)}, f32[64]{0:T(128)}, u32[]{:S(2)}) copy-start(f32[64]{0:T(128)} %get-tuple-element.91) | copy-start | bytes 772
  64.6 3.2 %copy-start.16 = (f32[64]{0:T(128)S(1)}, f32[64]{0:T(128)}, u32[]{:S(2)}) copy-start(f32[64]{0:T(128)} %get-tuple-element.92) | copy-start | bytes 772
  64.6 3.2 %copy-start.17 = (f32[64]{0:T(128)S(1)}, f32[64]{0:T(128)}, u32[]{:S(2)}) copy-start(f32[64]{0:T(128)} %get-tuple-element.93) | copy-start | bytes 772
  64.6 3.2 %copy-start.18 = (f32[64]{0:T(128)S(1)}, f32[64]{0:T(128)}, u32[]{:S(2)}) copy-start(f32[64]{0:T(128)} %get-tuple-element.94) | copy-start | bytes 772
  67.7 6.9 %copy-start.8 = (bf16[2,48,32,64]{3,2,1,0:T(8,128)(2,1)}, bf16[2,48,32,64]{3,2,1,0:T(8,128)(2,1)S(1)}, u32[]{:S(2)}) copy-start(bf16[2,48,32,64]{3,2,1,0:T(8,128)(2,1)S(1)} %fusion.63) | copy-start | bytes 1179652
  71.3 3.4 %copy-start.10 = (bf16[2,48,32,64]{3,2,1,0:T(8,128)(2,1)}, bf16[2,48,32,64]{3,2,1,0:T(8,128)(2,1)S(1)}, u32[]{:S(2)}) copy-start(bf16[2,48,32,64]{3,2,1,0:T(8,128)(2,1)S(1)} %fusion.45) | copy-start | bytes 1179652
  74.6 3.4 %copy-start.12 = (bf16[2,48,32,64]{3,2,1,0:T(8,128)(2,1)}, bf16[2,48,32,64]{3,2,1,0:T(8,128)(2,1)S(1)}, u32[]{:S(2)}) copy-start(bf16[2,48,32,64]{3,2,1,0:T(8,128)(2,1)S(1)} %fusion.27) | copy-start | bytes 1179652
  74.6 6.0 %copy-start.14 = (bf16[256,227]{0,1:T(8,128)(2,1)S(1)}, bf16[256,227]{0,1:T(8,128)(2,1)}, u32[]{:S(2)}) copy-start(bf16[256,227]{0,1:T(8,128)(2,1)} %param.13) | copy-start | bytes 348676
  86.4 5.2 %copy-start.7 = (bf16[2,48,32,64]{3,2,1,0:T(8,128)(2,1)S(1)}, bf16[2,48,32,64]{3,2,1,0:T(8,128)(2,1)}, u32[]{:S(2)}) copy-start(bf16[2,48,32,64]{3,2,1,0:T(8,128)(2,1)} %copy-done.6) | copy-start | bytes 1179652
  86.4 5.2 %copy-start.9 = (bf16[2,48,32,64]{3,2,1,0:T(8,128)(2,1)S(1)}, bf16[2,48,32,64]{3,2,1,0:T(8,128)(2,1)}, u32[]{:S(2)}) copy-start(bf16[2,48,32,64]{3,2,1,0:T(8,128)(2,1)} %copy-done.8) | copy-start | bytes 1179652
  86.4 5.2 %copy-start.11 = (bf16[2,48,32,64]{3,2,1,0:T(8,128)(2,1)S(1)}, bf16[2,48,32,64]{3,2,1,0:T(8,128)(2,1)}, u32[]{:S(2)}) copy-start(bf16[2,48,32,64]{3,2,1,0:T(8,128)(2,1)} %copy-done.10) | copy-start | bytes 1179652
  86.4 5.2 %copy-start.13 = (bf16[2,48,32,64]{3,2,1,0:T(8,128)(2,1)S(1)}, bf16[2,48,32,64]{3,2,1,0:T(8,128)(2,1)}, u32[]{:S(2)}) copy-start(bf16[2,48,32,64]{3,2,1,0:T(8,128)(2,1)} %copy-done.12) | copy-start | bytes 1179652
  90.5 1.1 copy-start.5
  97.5 96.6 %all-reduce.7.cloned.1.call-start = ((), (), s32[]{:S(2)}) async-start(), calls=%async_computation.3 | async-start | bytes 999424 | tf_op jit(solution)/shard_map/psum | solution.py:13
Sparse Core Ops, SparseCore 0:
  97.6 19.8 all-reduce.8
  121.1 72.9 all-reduce.6
